TPU v7x, 32 devices: a whole 2x2x4 slice. The times are simulated.
32 devices in a mesh: req: 4 (over x, core), head: 8 (over z, y).
Axes of the slice: x: 2, y: 2, z: 4, core: 2. Of those that a mesh axis runs over, the one named last changes fastest.
Arguments:
- stretch_acts: bfloat16 [8, 256, 2048], P(None, ('req', 'head')), may hold values from -6 to 6
- cache_prefill: bfloat16 [8, 8, 256, 32, 128], P('req', None, 'head'), may hold values from -600 to 600
- stretch_lens: int32 [8], replicated, may hold values from 1 to 256, 1280 in all
- prefix_lens: int32 [8], replicated, may hold values from 1 to 256, 1280 in all
- req_order: int32 [8], replicated, may hold values from 0 to 7, each once
- attn_gain: bfloat16 [2048], replicated, may hold values from 0.25 to 1.75
- in_weight: bfloat16 [2048, 32, 192], P(None, 'head'), may hold values from -0.125 to 0.125
- slopes: float32 [32], P('head'), may hold values from 0.00390625 to 0.5
- out_weight: bfloat16 [32, 64, 2048], P('head'), may hold values from -0.125 to 0.125
- mlp_gain: bfloat16 [2048], replicated, may hold values from 0.25 to 1.75
- up_weight: bfloat16 [2048, 8192], P(None, 'head'), may hold values from -0.125 to 0.125
- down_weight: bfloat16 [8192, 2048], P('head'), may hold values from -0.0625 to 0.0625
Outputs:
- layer_out: bfloat16 [8, 256, 2048], P(None, ('req', 'head'))
- cache_decode: bfloat16 [8, 8, 256, 32, 128], P(None, 'req', None, 'head')
Inputs may be any that keep to these rules, and one draw needn't show every extreme that they name: `stretch_lens`: the entries sum to 1280 and the largest is exactly 256. `prefix_lens`: the entries sum to 1280 and the largest is exactly 256. `req_order`: each request appears once.
All inputs are finite; a program needn't handle non-finite values.
Results may differ from a plain program's by a relative error of at most 0.013.
The roundings to bfloat16 on the way count: a program that leaves them out, or rounds other values in their place, can miss the bound.
Values may be sent and summed in bfloat16 or wider, within the bound.
No kernel may reach another device: no remote copies, remote signals or barrier semaphores. Data moves between devices by JAX's collectives and lax.ppermute only.
A program may use at most 128 MiB of HBM per device.

v0:
```python
import math
import jax
import jax.numpy as jnp
from jax import lax
from jax.sharding import PartitionSpec as P

EPSILON = 1e-05


def layer_norm(values, gain):
    average = jnp.mean(values, axis=-1, keepdims=True)
    centred = values - average
    variance = jnp.mean(centred * centred, axis=-1, keepdims=True)
    return centred * lax.rsqrt(variance + EPSILON) * gain.astype(jnp.float32)


def attend(queries, pairs, prefix_len, slopes, head_dim):
    stretch = queries.shape[0]
    prefix = pairs.shape[0] - stretch
    keys_part = pairs[..., :head_dim]
    values_part = pairs[..., head_dim:]
    scores = jnp.einsum("qhd,khd->hqk", queries, keys_part, preferred_element_type=jnp.float32) * (
        1.0 / math.sqrt(head_dim)
    )
    row_index = jnp.arange(stretch, dtype=jnp.int32)
    key_index = jnp.arange(prefix + stretch, dtype=jnp.int32)
    in_prefix = key_index < prefix
    query_pos = prefix_len + row_index
    key_pos = jnp.where(in_prefix, key_index, prefix_len + key_index - prefix)
    allowed = jnp.where(
        in_prefix[None, :],
        key_index[None, :] < prefix_len,
        (key_index - prefix)[None, :] <= row_index[:, None],
    )
    distance = (query_pos[:, None] - key_pos[None, :]).astype(jnp.float32)
    scores = scores - slopes[:, None, None] * distance[None]
    scores = jnp.where(allowed[None], scores, -jnp.inf)
    highest = jnp.max(scores, axis=-1, keepdims=True)
    expo = jnp.exp(scores - highest)
    soft = (expo / jnp.sum(expo, axis=-1, keepdims=True)).astype(jnp.bfloat16)
    context = jnp.einsum("hqk,khd->qhd", soft, values_part, preferred_element_type=jnp.float32)
    return context.astype(jnp.bfloat16).reshape(stretch, -1)


def local(
    stretch_acts,
    cache_prefill,
    stretch_lens,
    prefix_lens,
    req_order,
    attn_gain,
    in_weight,
    slopes,
    out_weight,
    mlp_gain,
    up_weight,
    down_weight,
):
    req_count = lax.axis_size("req")
    head_count = lax.axis_size("head")
    req_index = lax.axis_index("req")
    head_index = lax.axis_index("head")
    requests = stretch_acts.shape[0]
    stretch_rows = stretch_acts.shape[1]
    features = stretch_acts.shape[2]
    group_size = requests // req_count
    span_rows = head_count * stretch_rows
    stretch_max = req_count * span_rows
    prefix_rows = cache_prefill.shape[2]
    heads_here = in_weight.shape[1]
    pair_width = cache_prefill.shape[4]
    head_dim = pair_width // 2
    members = lax.dynamic_slice_in_dim(req_order, req_index * group_size, group_size)
    member_stretch = jnp.take(stretch_lens, members)
    member_prefix = jnp.take(prefix_lens, members)
    ordered_prefix = jnp.take(prefix_lens, req_order)
    positions = head_index * prefix_rows + jnp.arange(prefix_rows, dtype=jnp.int32)
    keep = positions[None, :] < ordered_prefix[:, None]
    dealt_cache = jnp.where(
        keep[None, :, :, None, None],
        jnp.take(cache_prefill, req_order, axis=1),
        jnp.zeros((), cache_prefill.dtype),
    )
    relaid = lax.all_to_all(
        lax.all_to_all(dealt_cache, "head", split_axis=3, concat_axis=2, tiled=True),
        "req",
        split_axis=1,
        concat_axis=0,
        tiled=True,
    )
    current = relaid[0]
    dealt_acts = jnp.take(stretch_acts, req_order, axis=0)
    dealt_rows = lax.all_to_all(dealt_acts, "req", split_axis=0, concat_axis=1, tiled=True).reshape(
        group_size, req_count, stretch_rows, features
    )
    gathered = lax.all_gather(dealt_rows, "head", axis=2, tiled=True)
    normed = (
        layer_norm(gathered.astype(jnp.float32), attn_gain)
        .astype(jnp.bfloat16)
        .reshape(group_size * stretch_max, features)
    )
    mixed = jnp.dot(
        normed,
        in_weight.reshape(features, heads_here * 3 * head_dim),
        preferred_element_type=jnp.float32,
    )
    mixed = mixed.reshape(group_size, stretch_max, heads_here, 3 * head_dim).astype(jnp.bfloat16)
    contexts = []
    for member in range(group_size):
        pairs = jnp.concatenate([current[member], mixed[member, :, :, head_dim:]], axis=0)
        contexts.append(
            attend(mixed[member, :, :, :head_dim], pairs, member_prefix[member], slopes, head_dim)
        )
    context = jnp.concatenate(contexts, axis=0)
    partial_attn = jnp.dot(
        context,
        out_weight.reshape(heads_here * head_dim, features),
        preferred_element_type=jnp.float32,
    )
    partial_attn = partial_attn.reshape(group_size, req_count, span_rows, features)
    attn_rows = lax.psum_scatter(
        partial_attn.astype(jnp.bfloat16), "head", scatter_dimension=2, tiled=True
    ).astype(jnp.float32)
    residual_rows = dealt_rows.astype(jnp.float32) + attn_rows
    normed_rows = layer_norm(residual_rows, mlp_gain).astype(jnp.bfloat16)
    normed_all = lax.all_gather(normed_rows, "head", axis=2, tiled=True)
    inner = jax.nn.gelu(
        jnp.dot(
            normed_all.reshape(group_size * stretch_max, features),
            up_weight,
            preferred_element_type=jnp.float32,
        ),
        approximate=False,
    ).astype(jnp.bfloat16)
    partial_mlp = jnp.dot(inner, down_weight, preferred_element_type=jnp.float32).reshape(
        group_size, req_count, span_rows, features
    )
    mlp_rows = lax.psum_scatter(
        partial_mlp.astype(jnp.bfloat16), "head", scatter_dimension=2, tiled=True
    ).astype(jnp.float32)
    row_number = (
        jnp.arange(req_count, dtype=jnp.int32)[:, None] * head_count + head_index
    ) * stretch_rows + jnp.arange(stretch_rows, dtype=jnp.int32)[None, :]
    usable = row_number[None] < member_stretch[:, None, None]
    result = jnp.where(
        usable[..., None], residual_rows + mlp_rows, jnp.zeros((), jnp.float32)
    ).astype(jnp.bfloat16)
    returned = lax.all_to_all(result, "req", split_axis=1, concat_axis=0, tiled=True).reshape(
        requests, stretch_rows, features
    )
    inverse = jnp.argsort(req_order)
    layer_out = jnp.take(returned, inverse, axis=0)
    return (layer_out, relaid)


def solution(mesh):
    return jax.shard_map(
        local,
        mesh=mesh,
        in_specs=(
            P(None, ("req", "head"), None),
            P("req", None, "head", None, None),
            P(),
            P(),
            P(),
            P(),
            P(None, "head", None),
            P("head"),
            P("head", None, None),
            P(),
            P(None, "head"),
            P("head", None),
        ),
        out_specs=(P(None, ("req", "head"), None), P(None, "req", None, "head", None)),
        check_vma=False,
    )
```

profile of v0, /device:TPU:1, one launch (start us, length us, event | category | flops | bytes accessed | tf_op | source)
XLA Modules:
  0.0 463.2 jit_solution(14605150824195133511)
XLA Ops:
  7.2 0.8 compare_select_fusion.1
  8.0 1.4 gather_fusion
  9.4 0.7 broadcast_select_fusion.4
  10.1 1.5 gather_fusion.3
  11.6 0.8 broadcast_select_fusion.1
  12.4 4.3 all-to-all-start
  16.7 5.3 %gather_fusion.1 = bf16[8,2,32,32,128]{4,3,2,1,0:T(8,128)(2,1)} fusion(bf16[2,8,32,32,128]{4,3,2,1,0:T(8,128)(2,1)} %param.17, s32[1024]{0:T(1024)S(1)} %pad_clamp_fusion.1), kind=kCustom, calls=%fused_computation.5 | custom fusion | bytes 8388640 | tf_op jit(solution)/shard_map/jit(_take)/gather | solution.py:81
  22.0 2.6 select_bitcast_fusion
  24.6 3.6 copy.44
  28.3 0.7 copy-done.5
  29.0 6.2 %all-to-all-start.1 = ((bf16[2,8,32,32,128]{4,2,0,1,3:T(8,128)(2,1)}), bf16[2,8,32,32,128]{4,2,0,1,3:T(8,128)(2,1)}, u32[]{:S(2)}, u32[]{:S(2)}) async-start(bf16[2,8,32,32,128]{4,2,0,1,3:T(8,128)(2,1)} %copy.44), calls=%async_computation.1 | async-start | bytes 8388608 | tf_op jit(solution)/shard_map/all_to_all | solution.py:85
  35.2 0.7 all-gather.3.cloned.1.call-update
  36.0 0.6 gather_fusion.4
  36.6 0.6 gather_fusion.2
  37.3 0.6 fusion.118
  38.0 0.6 iota_add_fusion.3
  38.6 1.3 iota_compare_fusion.1
  39.9 0.6 iota_add_fusion.2
  40.5 0.6 add_select_fusion.1
  41.2 112.4 %all-to-all-done.1 = bf16[2,8,32,32,128]{4,2,0,1,3:T(8,128)(2,1)} async-done(((bf16[2,8,32,32,128]{4,2,0,1,3:T(8,128)(2,1)}), bf16[2,8,32,32,128]{4,2,0,1,3:T(8,128)(2,1)}, u32[]{:S(2)}, u32[]{:S(2)}) %all-to-all-start.1) | async-done | bytes 4194336 | tf_op jit(solution)/shard_map/all_to_all | solution.py:85
  153.5 3.5 copy.46
  157.0 2.3 copy.47
  159.3 5.9 %all-to-all-start.2 = ((bf16[2,8,256,4,128]{4,2,3,0,1:T(8,128)(2,1)}), bf16[2,8,256,4,128]{4,2,3,0,1:T(8,128)(2,1)}, u32[]{:S(2)}, u32[]{:S(2)}) async-start(bf16[2,8,256,4,128]{4,2,3,0,1:T(8,128)(2,1)} %copy.47), calls=%async_computation.2 | async-start | bytes 8388608 | tf_op jit(solution)/shard_map/all_to_all | solution.py:84
  165.3 0.6 add_select_fusion
  165.9 0.8 fusion.54
  166.7 1.0 subtract_convert_fusion.1
  167.6 0.9 subtract_convert_fusion
  168.6 2.1 convert_reduce_fusion
  170.8 0.7 fusion.4
  171.5 0.7 fusion.6
  172.2 0.1 copy.50
  172.4 1.8 fusion.19
  174.2 0.9 copy-done.11
  175.1 37.5 %all-to-all-done.2 = bf16[2,8,256,4,128]{4,2,3,0,1:T(8,128)(2,1)} async-done(((bf16[2,8,256,4,128]{4,2,3,0,1:T(8,128)(2,1)}), bf16[2,8,256,4,128]{4,2,3,0,1:T(8,128)(2,1)}, u32[]{:S(2)}, u32[]{:S(2)}) %all-to-all-start.2) | async-done | bytes 4194336 | tf_op jit(solution)/shard_map/all_to_all | solution.py:84
  212.7 7.4 %copy.49 = bf16[4,2,2,256,4,128]{3,5,4,2,1,0:T(8,128)(2,1)} copy(bf16[4,2,2,256,4,128]{5,3,4,1,2,0:T(8,128)(2,1)} %bitcast.9) | data formatting | bytes 8388608 | tf_op jit(solution)/shard_map/all_to_all | solution.py:84
  220.1 1.1 slice_bitcast_fusion.3
  221.2 1.1 fusion.120
  222.2 1.9 convolution_convert_fusion.3
  224.1 1.1 fusion.119
  225.2 1.2 convolution_convert_fusion.2
  226.6 0.7 convolution_convert_fusion.1
  227.4 2.9 copy.74
  230.3 4.5 reshape.419
  234.8 0.3 all-gather.5.cloned.1.call-start
  235.1 0.4 copy-done.16
  235.5 63.5 %reduce-scatter.7.cloned.1.call-done = bf16[8,16384]{1,0:T(8,128)(2,1)} async-done(((bf16[64,16384]{1,0:T(8,128)(2,1)}), bf16[8,16384]{1,0:T(8,128)(2,1)}) %reduce-scatter.7.cloned.1.call-update) | async-done | bytes 262160
  299.0 1.1 reshape.420
  300.2 0.3 fusion.55
  300.5 0.3 multiply_reduce_fusion
  300.8 0.9 multiply_convert_fusion
  301.8 49.1 %all-gather.5.cloned.1.call-done = bf16[2,4,64,2048]{3,2,0,1:T(8,128)(2,1)} async-done(((bf16[2,4,8,2048]{3,2,0,1:T(8,128)(2,1)}), bf16[2,4,64,2048]{3,2,0,1:T(8,128)(2,1)}) %all-gather.5.cloned.1.call-update) | async-done | bytes 2097168 | tf_op jit(solution)/shard_map/all_gather | solution.py:126
  350.9 1.8 copy.53
  352.7 13.7 %convolution_convert_fusion = bf16[512,2048]{1,0:T(8,128)(2,1)} fusion(bf16[1024,2048]{1,0:T(8,128)(2,1)} %param.27, bf16[512,2048]{1,0:T(8,128)(2,1)S(1)} %bitcast.113, bf16[2048,1024]{1,0:T(8,128)(2,1)} %param.26), kind=kOutput, calls=%fused_computation.19 | convolution fusion | flops 4330094592 | bytes 12582912 | tf_op jit(solution)/shard_map/dot_general | solution.py:135
  366.4 3.2 copy.73
  369.6 2.8 reshape.421
  372.4 1.0 sort.17
  373.6 64.4 %reduce-scatter.9.cloned.1.call-done = bf16[8,16384]{1,0:T(8,128)(2,1)} async-done(((bf16[64,16384]{1,0:T(8,128)(2,1)}), bf16[8,16384]{1,0:T(8,128)(2,1)}) %reduce-scatter.9.cloned.1.call-update) | async-done | bytes 262160
  438.0 1.1 reshape.422
  439.1 1.0 select_convert_fusion
  440.2 5.9 %all-to-all-start.3 = ((bf16[2,4,8,2048]{3,2,0,1:T(8,128)(2,1)}), bf16[2,4,8,2048]{3,2,0,1:T(8,128)(2,1)S(1)}, u32[]{:S(2)}, u32[]{:S(2)}) async-start(bf16[2,4,8,2048]{3,2,0,1:T(8,128)(2,1)} %select_convert_fusion), calls=%async_computation.3 | async-start | bytes 524288 | tf_op jit(solution)/shard_map/all_to_all | solution.py:148
  446.1 7.6 %copy.55 = bf16[8,2,256,4,128]{4,3,2,1,0:T(4,128)(2,1)} copy(bf16[8,2,256,4,128]{2,4,3,1,0:T(8,128)(2,1)} %bitcast.101) | data formatting | bytes 8388608
  453.6 0.7 copy-done.7
  454.4 1.5 gather_fusion.5
  455.9 0.8 broadcast_select_fusion
  (67 shorter events, 1.0 us)
Async XLA Ops:
  7.2 165.2 %copy-start = (bf16[2048,4,192]{0,2,1:T(8,128)(2,1)S(1)}, bf16[2048,4,192]{0,2,1:T(8,128)(2,1)}, u32[]{:S(2)}) copy-start(bf16[2048,4,192]{0,2,1:T(8,128)(2,1)} %param.22) | copy-start | bytes 9437188
  12.4 15.8 %all-to-all-start = ((bf16[8,8,2048]{2,1,0:T(8,128)(2,1)}), bf16[8,8,2048]{2,1,0:T(8,128)(2,1)S(1)}, u32[]{:S(2)}, u32[]{:S(2)}) async-start(bf16[8,8,2048]{2,1,0:T(8,128)(2,1)} %broadcast_select_fusion.1), calls=%async_computation | async-start | bytes 524288 | tf_op jit(solution)/shard_map/all_to_all | solution.py:93
  28.2 7.6 %copy-start.17 = (s32[8]{0:T(128)S(1)}, s32[8]{0:T(128)}, u32[]{:S(2)}) copy-start(s32[8]{0:T(128)} %param.20) | copy-start | bytes 100
  28.2 7.7 %copy-start.2 = (s32[8]{0:T(128)S(1)}, s32[8]{0:T(128)}, u32[]{:S(2)}) copy-start(s32[8]{0:T(128)} %param.19) | copy-start | bytes 100
  28.2 8.4 %copy-start.3 = (s32[8]{0:T(128)S(1)}, s32[8]{0:T(128)}, u32[]{:S(2)}) copy-start(s32[8]{0:T(128)} %param.18) | copy-start | bytes 100
  28.2 9.0 %copy-start.15 = (bf16[2048]{0:T(1024)(128)(2,1)S(1)}, bf16[2048]{0:T(1024)(128)(2,1)}, u32[]{:S(2)}) copy-start(bf16[2048]{0:T(1024)(128)(2,1)} %param.21) | copy-start | bytes 12292
  28.3 0.7 copy-start.5
  29.0 124.6 %all-to-all-start.1 = ((bf16[2,8,32,32,128]{4,2,0,1,3:T(8,128)(2,1)}), bf16[2,8,32,32,128]{4,2,0,1,3:T(8,128)(2,1)}, u32[]{:S(2)}, u32[]{:S(2)}) async-start(bf16[2,8,32,32,128]{4,2,0,1,3:T(8,128)(2,1)} %copy.44), calls=%async_computation.1 | async-start | bytes 8388608 | tf_op jit(solution)/shard_map/all_to_all | solution.py:85
  35.1 133.5 %all-gather.3.cloned.1.call-start = ((), (), s32[]{:S(2)}) async-start(), calls=%async_computation.6 | async-start | bytes 2359296 | tf_op jit(solution)/shard_map/all_gather | solution.py:96
  159.3 53.4 %all-to-all-start.2 = ((bf16[2,8,256,4,128]{4,2,3,0,1:T(8,128)(2,1)}), bf16[2,8,256,4,128]{4,2,3,0,1:T(8,128)(2,1)}, u32[]{:S(2)}, u32[]{:S(2)}) async-start(bf16[2,8,256,4,128]{4,2,3,0,1:T(8,128)(2,1)} %copy.47), calls=%async_computation.2 | async-start | bytes 8388608 | tf_op jit(solution)/shard_map/all_to_all | solution.py:84
  165.3 133.7 %reduce-scatter.7.cloned.1.call-start = ((), (), s32[]{:S(2)}) async-start(), calls=%async_computation.8 | async-start | bytes 2359296
  168.6 2.2 copy-start.4
  174.2 0.9 copy-start.11
  212.7 8.5 %copy-start.10 = (f32[256,512]{1,0:T(8,128)S(1)}, f32[256,512]{1,0:T(8,128)}, u32[]{:S(2)}) copy-start(f32[256,512]{1,0:T(8,128)} %subtract_convert_fusion.1) | copy-start | bytes 1572868
  212.7 8.5 %copy-start.12 = (bf16[2,256,4,192]{1,3,2,0:T(8,128)(2,1)S(1)}, bf16[2,256,4,192]{1,3,2,0:T(8,128)(2,1)}, u32[]{:S(2)}) copy-start(bf16[2,256,4,192]{1,3,2,0:T(8,128)(2,1)} %copy-done.11) | copy-start | bytes 2359300
  212.7 8.5 %copy-start.13 = (pred[256,512]{1,0:T(8,128)(4,1)S(1)}, pred[256,512]{1,0:T(8,128)(4,1)}, u32[]{:S(2)}) copy-start(pred[256,512]{1,0:T(8,128)(4,1)} %get-tuple-element.24) | copy-start | bytes 393220
  212.7 8.5 %copy-start.18 = (f32[4]{0:T(128)S(1)}, f32[4]{0:T(128)}, u32[]{:S(2)}) copy-start(f32[4]{0:T(128)} %param.23) | copy-start | bytes 52
  222.2 1.9 copy-start.9
  225.2 1.3 copy-start.14
  225.2 1.4 copy-start.8
  234.8 0.7 copy-start.16
  234.8 65.4 %copy-start.6 = (bf16[8,8,2048]{2,1,0:T(8,128)(2,1)S(1)}, bf16[8,8,2048]{2,1,0:T(8,128)(2,1)}, u32[]{:S(2)}) copy-start(bf16[8,8,2048]{2,1,0:T(8,128)(2,1)} %copy-done.5) | copy-start | bytes 786436
  234.8 116.1 %all-gather.5.cloned.1.call-start = ((), (), s32[]{:S(2)}) async-start(), calls=%async_computation.7 | async-start | bytes 2359296 | tf_op jit(solution)/shard_map/all_gather | solution.py:126
  301.7 136.3 %reduce-scatter.9.cloned.1.call-start = ((), (), s32[]{:S(2)}) async-start(), calls=%async_computation.9 | async-start | bytes 2359296
  440.2 13.5 %all-to-all-start.3 = ((bf16[2,4,8,2048]{3,2,0,1:T(8,128)(2,1)}), bf16[2,4,8,2048]{3,2,0,1:T(8,128)(2,1)S(1)}, u32[]{:S(2)}, u32[]{:S(2)}) async-start(bf16[2,4,8,2048]{3,2,0,1:T(8,128)(2,1)} %select_convert_fusion), calls=%async_computation.3 | async-start | bytes 524288 | tf_op jit(solution)/shard_map/all_to_all | solution.py:148
  446.1 10.6 %copy-start.1 = (bf16[2048,4,192]{0,2,1:T(8,128)(2,1)S(1)}, bf16[2048,4,192]{0,2,1:T(8,128)(2,1)}, u32[]{:S(2)}) copy-start(bf16[2048,4,192]{0,2,1:T(8,128)(2,1)} %param.22) | copy-start | bytes 9437188
  453.6 0.7 copy-start.7
Sparse Core Ops, SparseCore 0:
  38.7 103.0 all-gather.2
  234.9 64.0 reduce-scatter.6
  301.9 49.0 all-gather.4
  372.6 65.4 reduce-scatter.8
where the time goes:
time: 464 us; the launch traced here: 463 us
  waiting for transfers between devices  328 us (71%)
  local copies, waits for them, and re-layouts  57.7 us (12%)
  starting transfers between devices  22.6 us (5%)
  matrix products  21.5 us (5%)
  other arithmetic  19.6 us (4%)
  between operations  14.1 us (3%)
    unnamed x6, waiting for transfers between devices  129 us
    all_to_all x1, waiting for transfers between devices, local(): lax.all_to_all(dealt_cache, 'head', split_axis=3, concat_axis=2, tiled=True)  112 us
    all_gather x1, waiting for transfers between devices, local(): normed_all = lax.all_gather(normed_rows, 'head', axis=2, tiled=True)  49.1 us
    all_to_all x1, waiting for transfers between devices, local(): lax.all_to_all(lax.all_to_all(dealt_cache, 'head', split_axis=3, concat_a...  37.5 us
    unnamed x45, local copies, waits for them, and re-layouts  26.1 us
    dot_general x1, matrix products, local(): jnp.dot(inner, down_weight, preferred_element_type=jnp.float32)  13.7 us
  transfers between devices with their start and end apart: 8, of which 5 were waited for; matrix products, arithmetic and copies ran while one was open for 9% of the time, Pallas kernels for 0%

commit v1 on v0

--- a/solution.py
+++ b/solution.py
@@ -1,3 +1,4 @@
+import functools
 import math
 import jax
 import jax.numpy as jnp
@@ -5,6 +6,38 @@
 from jax.sharding import PartitionSpec as P
 
 EPSILON = 1e-05
+
+
+def supply_all_outputs(work_x, where_dim, panel):
+    item_now, base_arr = (work_x.shape[:where_dim], work_x.shape[where_dim + 1 :])
+    res = work_x.reshape(*item_now, panel, -1, *base_arr)
+    return jnp.moveaxis(res, where_dim, 0)
+
+
+def screen_process(state, axis_no):
+    state = jnp.moveaxis(state, 0, axis_no)
+    view_out = state.shape
+    return state.reshape(
+        *view_out[:axis_no], view_out[axis_no] * view_out[axis_no + 1], *view_out[axis_no + 2 :]
+    )
+
+
+def slices_direct(own_rows, lane_axis, arr_in, mat):
+    taken_in = lax.psum(1, lane_axis)
+    z2 = lax.axis_index(lane_axis)
+    tmp, t1 = (taken_in, z2)
+    long_array = supply_all_outputs(own_rows, arr_in, tmp)
+    blocks_here = [long_array[t1]]
+    for dd in range(1, tmp):
+        carry_in = long_array[t1 ^ dd]
+        h_now = lax.ppermute(carry_in, lane_axis, [(i, i ^ dd) for i in range(tmp)])
+        blocks_here.append(h_now)
+    far_arr = jnp.stack(blocks_here)
+    long_array = far_arr[t1 ^ jnp.arange(tmp)]
+    return screen_process(long_array, mat)
+
+
+resolve_spot = functools.partial(slices_direct, lane_axis="head", arr_in=3, mat=2)
 
 
 def layer_norm(values, gain):
@@ -82,11 +115,7 @@
         jnp.zeros((), cache_prefill.dtype),
     )
     relaid = lax.all_to_all(
-        lax.all_to_all(dealt_cache, "head", split_axis=3, concat_axis=2, tiled=True),
-        "req",
-        split_axis=1,
-        concat_axis=0,
-        tiled=True,
+        resolve_spot(dealt_cache), "req", split_axis=1, concat_axis=0, tiled=True
     )
     current = relaid[0]
     dealt_acts = jnp.take(stretch_acts, req_order, axis=0)

time: 464 us -> 474 us (1.022)
  waiting for transfers between devices: 328 us -> 299 us
  local copies, waits for them, and re-layouts: 57.7 us -> 75.9 us
  starting transfers between devices: 22.6 us -> 37.7 us
    all_to_all x2 -> x1, waiting for transfers between devices: 150 us -> 38.9 us  [local(): lax.all_to_all(resolve_spot(dealt_cache), 'req', split_axis=1, concat_axi...]
    ppermute x0 -> x7, waiting for transfers between devices: none -> 42.5 us  [slices_direct(): h_now = lax.ppermute(carry_in, lane_axis, [(i, i ^ dd) for i in range(tmp)])]
    unnamed x6, waiting for transfers between devices: 129 us -> 165 us
    unnamed x45 -> x48, local copies, waits for them, and re-layouts: 26.1 us -> 38.9 us
    ppermute x0 -> x7, starting transfers between devices: none -> 11 us  [slices_direct(): h_now = lax.ppermute(carry_in, lane_axis, [(i, i ^ dd) for i in range(tmp)])]
    all_to_all x3 -> x1, local copies, waits for them, and re-layouts: 13.1 us -> 7.26 us  [local(): lax.all_to_all(resolve_spot(dealt_cache), 'req', split_axis=1, concat_axi...]
    gather x0 -> x1, local copies, waits for them, and re-layouts: none -> 5.28 us  [slices_direct(): long_array = far_arr[t1 ^ jnp.arange(tmp)]]
    all_to_all x2 -> x1, starting transfers between devices: 12.1 us -> 15.2 us  [local(): lax.all_to_all(resolve_spot(dealt_cache), 'req', split_axis=1, concat_axi...]
  transfers between devices with their start and end apart: 8 -> 14, of which waited for: 5 -> 9; matrix products, arithmetic and copies ran while one was open for 9% -> 11% of each run, Pallas kernels for 0% -> 0%
where the time goes in v1:
time: 474 us; the launch traced here: 472 us
  waiting for transfers between devices  299 us (63%)
  local copies, waits for them, and re-layouts  75.9 us (16%)
  starting transfers between devices  37.7 us (8%)
  matrix products  25.1 us (5%)
  other arithmetic  20.8 us (4%)
  between operations  14.1 us (3%)
    unnamed x6, waiting for transfers between devices  165 us
    all_gather x1, waiting for transfers between devices, local(): normed_all = lax.all_gather(normed_rows, 'head', axis=2, tiled=True)  49 us
    ppermute x7, waiting for transfers between devices, slices_direct(): h_now = lax.ppermute(carry_in, lane_axis, [(i, i ^ dd) for i in range(tmp)])  42.5 us
    unnamed x48, local copies, waits for them, and re-layouts  38.9 us
    all_to_all x1, waiting for transfers between devices, local(): lax.all_to_all(resolve_spot(dealt_cache), 'req', split_axis=1, concat_axi...  38.9 us
    all_to_all x1, starting transfers between devices, local(): lax.all_to_all(resolve_spot(dealt_cache), 'req', split_axis=1, concat_axi...  15.2 us
    dot_general x1, matrix products, local(): jnp.dot(inner, down_weight, preferred_element_type=jnp.float32)  13.7 us
    ppermute x7, starting transfers between devices, slices_direct(): h_now = lax.ppermute(carry_in, lane_axis, [(i, i ^ dd) for i in range(tmp)])  11 us
  transfers between devices with their start and end apart: 14, of which 9 were waited for; matrix products, arithmetic and copies ran while one was open for 11% of the time, Pallas kernels for 0%

profile of v1, /device:TPU:1, one launch (start us, length us, event | category | flops | bytes accessed | tf_op | source)
XLA Modules:
  0.0 472.4 jit_solution(5484144538942857736)
XLA Ops:
  7.2 0.8 compare_select_fusion.1
  8.0 1.4 gather_fusion
  10.1 5.3 %gather_fusion.1 = bf16[8,2,32,32,128]{4,3,2,1,0:T(8,128)(2,1)} fusion(bf16[2,8,32,32,128]{4,3,2,1,0:T(8,128)(2,1)} %param.17, s32[1024]{0:T(1024)S(1)} %pad_clamp_fusion.2), kind=kCustom, calls=%fused_computation.5 | custom fusion | bytes 8388640 | tf_op jit(solution)/shard_map/jit(_take)/gather | solution.py:114
  15.5 3.8 fusion.7
  19.3 2.4 dynamic-slice_bitcast_fusion
  21.7 0.7 copy-done.5
  22.4 2.1 collective-permute-start
  24.5 1.3 collective-permute-start.1
  25.8 2.4 collective-permute-start.3
  28.2 1.0 collective-permute-start.4
  29.2 1.5 gather_fusion.4
  30.7 0.8 broadcast_select_fusion.1
  31.5 5.4 %all-to-all-start = ((bf16[8,8,2048]{2,1,0:T(8,128)(2,1)}), bf16[8,8,2048]{2,1,0:T(8,128)(2,1)S(1)}, u32[]{:S(2)}, u32[]{:S(2)}) async-start(bf16[8,8,2048]{2,1,0:T(8,128)(2,1)} %broadcast_select_fusion.1), calls=%async_computation | async-start | bytes 524288 | tf_op jit(solution)/shard_map/all_to_all | solution.py:122
  37.0 1.9 bitcast_dynamic-update-slice_fusion.7
  38.9 3.4 all-to-all-done
  43.0 3.4 collective-permute-start.5
  46.4 1.9 bitcast_dynamic-update-slice_fusion.6
  48.3 14.1 %collective-permute-done.1 = bf16[2,8,32,4,128]{4,2,3,1,0:T(8,128)(2,1)} collective-permute-done((bf16[2,8,32,4,128]{4,2,3,1,0:T(8,128)(2,1)}, bf16[2,8,32,4,128]{4,2,3,1,0:T(8,128)(2,1)}, u32[]{:S(2)}, u32[]{:S(2)}) %collective-permute-start.1) | collective-permute-done | bytes 524320 | tf_op jit(solution)/shard_map/ppermute | solution.py:33
  62.3 0.8 collective-permute-start.6
  63.2 1.9 bitcast_dynamic-update-slice_fusion.5
  65.0 9.8 %collective-permute-done.2 = bf16[2,8,32,4,128]{4,2,3,1,0:T(8,128)(2,1)} collective-permute-done((bf16[2,8,32,4,128]{4,2,3,1,0:T(8,128)(2,1)}, bf16[2,8,32,4,128]{4,2,3,1,0:T(8,128)(2,1)}, u32[]{:S(2)}, u32[]{:S(2)}) %collective-permute-start.2) | collective-permute-done | bytes 524320 | tf_op jit(solution)/shard_map/ppermute | solution.py:33
  74.8 1.9 bitcast_dynamic-update-slice_fusion.4
  76.7 1.9 bitcast_dynamic-update-slice_fusion.3
  78.6 1.9 bitcast_dynamic-update-slice_fusion.2
  80.5 8.3 %collective-permute-done.5 = bf16[2,8,32,4,128]{4,2,3,1,0:T(8,128)(2,1)S(1)} collective-permute-done((bf16[2,8,32,4,128]{4,2,3,1,0:T(8,128)(2,1)}, bf16[2,8,32,4,128]{4,2,3,1,0:T(8,128)(2,1)S(1)}, u32[]{:S(2)}, u32[]{:S(2)}) %collective-permute-start.5) | collective-permute-done | bytes 524320 | tf_op jit(solution)/shard_map/ppermute | solution.py:33
  88.9 0.8 bitcast_dynamic-update-slice_fusion.1
  89.7 10.2 %collective-permute-done.6 = bf16[2,8,32,4,128]{4,2,3,1,0:T(8,128)(2,1)S(1)} collective-permute-done((bf16[2,8,32,4,128]{4,2,3,1,0:T(8,128)(2,1)}, bf16[2,8,32,4,128]{4,2,3,1,0:T(8,128)(2,1)S(1)}, u32[]{:S(2)}, u32[]{:S(2)}) %collective-permute-start.6) | collective-permute-done | bytes 524320 | tf_op jit(solution)/shard_map/ppermute | solution.py:33
  99.9 0.8 bitcast_dynamic-update-slice_fusion
  100.8 5.3 %gather_fusion.2 = bf16[8,2,8,32,4,128]{5,3,4,2,1,0:T(8,128)(2,1)} fusion(bf16[8,2,8,32,4,128]{5,3,4,2,1,0:T(8,128)(2,1)} %bitcast_dynamic-update-slice_fusion, s32[1024]{0:T(1024)S(1)} %pad_clamp_fusion.1), kind=kCustom, calls=%fused_computation.6 | custom fusion | bytes 8388640 | tf_op jit(solution)/shard_map/gather | solution.py:36
  106.0 3.4 copy.38
  109.5 2.3 copy.39
  111.8 15.2 %all-to-all-start.1 = ((bf16[2,8,256,4,128]{4,2,3,0,1:T(8,128)(2,1)}), bf16[2,8,256,4,128]{4,2,3,0,1:T(8,128)(2,1)}, u32[]{:S(2)}, u32[]{:S(2)}) async-start(bf16[2,8,256,4,128]{4,2,3,0,1:T(8,128)(2,1)} %copy.39), calls=%async_computation.1 | async-start | bytes 8388608 | tf_op jit(solution)/shard_map/all_to_all | solution.py:117
  129.7 1.3 iota_compare_fusion.1
  132.8 0.8 fusion.55
  133.6 0.9 subtract_convert_fusion.1
  134.5 0.9 subtract_convert_fusion
  135.4 38.9 %all-to-all-done.1 = bf16[2,8,256,4,128]{4,2,3,0,1:T(8,128)(2,1)} async-done(((bf16[2,8,256,4,128]{4,2,3,0,1:T(8,128)(2,1)}), bf16[2,8,256,4,128]{4,2,3,0,1:T(8,128)(2,1)}, u32[]{:S(2)}, u32[]{:S(2)}) %all-to-all-start.1) | async-done | bytes 4194336 | tf_op jit(solution)/shard_map/all_to_all | solution.py:117
  174.3 7.3 %copy.41 = bf16[4,2,2,256,4,128]{3,5,4,2,1,0:T(8,128)(2,1)} copy(bf16[4,2,2,256,4,128]{5,3,4,1,2,0:T(8,128)(2,1)} %bitcast.24) | data formatting | bytes 8388608 | tf_op jit(solution)/shard_map/all_to_all | solution.py:117
  181.6 1.8 slice_bitcast_fusion.3
  183.4 2.1 convert_reduce_fusion
  187.2 1.8 fusion.20
  189.0 0.9 copy-done.11
  189.9 2.3 fusion.122
  192.3 2.4 convolution_convert_fusion.3
  194.7 2.0 fusion.121
  196.7 2.2 convolution_convert_fusion.2
  199.8 2.9 copy.68
  202.8 4.5 reshape.464
  207.9 100.4 %reduce-scatter.7.cloned.1.call-done = bf16[8,16384]{1,0:T(8,128)(2,1)} async-done(((bf16[64,16384]{1,0:T(8,128)(2,1)}), bf16[8,16384]{1,0:T(8,128)(2,1)}) %reduce-scatter.7.cloned.1.call-update) | async-done | bytes 262160
  308.3 1.1 reshape.465
  310.1 0.9 multiply_convert_fusion
  311.1 49.0 %all-gather.5.cloned.1.call-done = bf16[2,4,64,2048]{3,2,0,1:T(8,128)(2,1)} async-done(((bf16[2,4,8,2048]{3,2,0,1:T(8,128)(2,1)}), bf16[2,4,64,2048]{3,2,0,1:T(8,128)(2,1)}) %all-gather.5.cloned.1.call-update) | async-done | bytes 2097168 | tf_op jit(solution)/shard_map/all_gather | solution.py:155
  360.1 1.8 copy.45
  362.0 13.7 %convolution_convert_fusion = bf16[512,2048]{1,0:T(8,128)(2,1)} fusion(bf16[1024,2048]{1,0:T(8,128)(2,1)} %param.27, bf16[512,2048]{1,0:T(8,128)(2,1)S(1)} %bitcast.146, bf16[2048,1024]{1,0:T(8,128)(2,1)} %param.26), kind=kOutput, calls=%fused_computation.21 | convolution fusion | flops 4330094592 | bytes 12582912 | tf_op jit(solution)/shard_map/dot_general | solution.py:164
  375.6 3.2 copy.67
  378.8 2.8 reshape.466
  381.7 1.0 sort.17
  382.8 64.5 %reduce-scatter.9.cloned.1.call-done = bf16[8,16384]{1,0:T(8,128)(2,1)} async-done(((bf16[64,16384]{1,0:T(8,128)(2,1)}), bf16[8,16384]{1,0:T(8,128)(2,1)}) %reduce-scatter.9.cloned.1.call-update) | async-done | bytes 262160
  447.3 1.1 reshape.467
  448.4 1.0 select_convert_fusion
  449.4 5.8 %all-to-all-start.2 = ((bf16[2,4,8,2048]{3,2,0,1:T(8,128)(2,1)}), bf16[2,4,8,2048]{3,2,0,1:T(8,128)(2,1)S(1)}, u32[]{:S(2)}, u32[]{:S(2)}) async-start(bf16[2,4,8,2048]{3,2,0,1:T(8,128)(2,1)} %select_convert_fusion), calls=%async_computation.2 | async-start | bytes 524288 | tf_op jit(solution)/shard_map/all_to_all | solution.py:177
  455.2 7.6 %copy.47 = bf16[8,2,256,4,128]{4,3,2,1,0:T(4,128)(2,1)} copy(bf16[8,2,256,4,128]{2,4,3,1,0:T(8,128)(2,1)} %bitcast.132) | data formatting | bytes 8388608
  463.5 1.5 gather_fusion.6
  465.0 0.8 broadcast_select_fusion
  (86 shorter events, 11.0 us)
Async XLA Ops:
  7.2 180.0 %copy-start = (bf16[2048,4,192]{0,2,1:T(8,128)(2,1)S(1)}, bf16[2048,4,192]{0,2,1:T(8,128)(2,1)}, u32[]{:S(2)}) copy-start(bf16[2048,4,192]{0,2,1:T(8,128)(2,1)} %param.22) | copy-start | bytes 9437188
  19.3 3.1 copy-start.5
  22.4 20.6 %collective-permute-start = (bf16[2,8,32,4,128]{4,2,3,1,0:T(8,128)(2,1)}, bf16[2,8,32,4,128]{4,2,3,1,0:T(8,128)(2,1)}, u32[]{:S(2)}, u32[]{:S(2)}) collective-permute-start(bf16[2,8,32,4,128]{4,2,3,1,0:T(8,128)(2,1)} %get-tuple-element.26), channel_id=1, source_target_pairs={{0,1},{1,0},{2,3},{3,2},{4,5},{5,4},{6,7},{7,6},{8,9},{9,8},{10,11... | collective-permute-start | bytes 1572872 | tf_op jit(solution)/shard_map/ppermute | solution.py:33
  24.5 37.9 %collective-permute-start.1 = (bf16[2,8,32,4,128]{4,2,3,1,0:T(8,128)(2,1)}, bf16[2,8,32,4,128]{4,2,3,1,0:T(8,128)(2,1)}, u32[]{:S(2)}, u32[]{:S(2)}) collective-permute-start(bf16[2,8,32,4,128]{4,2,3,1,0:T(8,128)(2,1)} %get-tuple-element.25), channel_id=1, source_target_pairs={{0,2},{1,3},{2,0},{3,1},{4,6},{5,7},{6,4},{7,5},{8,10},{9,11},{10,... | collective-permute-start | bytes 1572872 | tf_op jit(solution)/shard_map/ppermute | solution.py:33
  25.8 49.0 %collective-permute-start.2 = (bf16[2,8,32,4,128]{4,2,3,1,0:T(8,128)(2,1)}, bf16[2,8,32,4,128]{4,2,3,1,0:T(8,128)(2,1)}, u32[]{:S(2)}, u32[]{:S(2)}) collective-permute-start(bf16[2,8,32,4,128]{4,2,3,1,0:T(8,128)(2,1)} %get-tuple-element.24), channel_id=1, source_target_pairs={{0,3},{1,2},{2,1},{3,0},{4,7},{5,6},{6,5},{7,4},{8,11},{9,10},{10,... | collective-permute-start | bytes 1572872 | tf_op jit(solution)/shard_map/ppermute | solution.py:33
  25.8 50.9 %collective-permute-start.3 = (bf16[2,8,32,4,128]{4,2,3,1,0:T(8,128)(2,1)}, bf16[2,8,32,4,128]{4,2,3,1,0:T(8,128)(2,1)}, u32[]{:S(2)}, u32[]{:S(2)}) collective-permute-start(bf16[2,8,32,4,128]{4,2,3,1,0:T(8,128)(2,1)} %get-tuple-element.23), channel_id=1, source_target_pairs={{0,4},{1,5},{2,6},{3,7},{4,0},{5,1},{6,2},{7,3},{8,12},{9,13},{10,... | collective-permute-start | bytes 1572872 | tf_op jit(solution)/shard_map/ppermute | solution.py:33
  28.2 50.4 %collective-permute-start.4 = (bf16[2,8,32,4,128]{4,2,3,1,0:T(8,128)(2,1)}, bf16[2,8,32,4,128]{4,2,3,1,0:T(8,128)(2,1)}, u32[]{:S(2)}, u32[]{:S(2)}) collective-permute-start(bf16[2,8,32,4,128]{4,2,3,1,0:T(8,128)(2,1)} %get-tuple-element.22), channel_id=1, source_target_pairs={{0,5},{1,4},{2,7},{3,6},{4,1},{5,0},{6,3},{7,2},{8,13},{9,12},{10,... | collective-permute-start | bytes 1572872 | tf_op jit(solution)/shard_map/ppermute | solution.py:33
  31.5 10.7 %all-to-all-start = ((bf16[8,8,2048]{2,1,0:T(8,128)(2,1)}), bf16[8,8,2048]{2,1,0:T(8,128)(2,1)S(1)}, u32[]{:S(2)}, u32[]{:S(2)}) async-start(bf16[8,8,2048]{2,1,0:T(8,128)(2,1)} %broadcast_select_fusion.1), calls=%async_computation | async-start | bytes 524288 | tf_op jit(solution)/shard_map/all_to_all | solution.py:122
  37.0 146.4 %all-gather.3.cloned.1.call-start = ((), (), s32[]{:S(2)}) async-start(), calls=%async_computation.5 | async-start | bytes 2359296 | tf_op jit(solution)/shard_map/all_gather | solution.py:125
  42.3 0.7 copy-start.6
  43.0 45.9 %collective-permute-start.5 = (bf16[2,8,32,4,128]{4,2,3,1,0:T(8,128)(2,1)}, bf16[2,8,32,4,128]{4,2,3,1,0:T(8,128)(2,1)S(1)}, u32[]{:S(2)}, u32[]{:S(2)}) collective-permute-start(bf16[2,8,32,4,128]{4,2,3,1,0:T(8,128)(2,1)} %get-tuple-element.21), channel_id=1, source_target_pairs={{0,6},{1,7},{2,4},{3,5},{4,2},{5,3},{6,0},{7,1},{8,14},{9,15},{10,... | collective-permute-start | bytes 1572872 | tf_op jit(solution)/shard_map/ppermute | solution.py:33
  62.3 37.6 %collective-permute-start.6 = (bf16[2,8,32,4,128]{4,2,3,1,0:T(8,128)(2,1)}, bf16[2,8,32,4,128]{4,2,3,1,0:T(8,128)(2,1)S(1)}, u32[]{:S(2)}, u32[]{:S(2)}) collective-permute-start(bf16[2,8,32,4,128]{4,2,3,1,0:T(8,128)(2,1)} %get-tuple-element.20), channel_id=1, source_target_pairs={{0,7},{1,6},{2,5},{3,4},{4,3},{5,2},{6,1},{7,0},{8,15},{9,14},{10,... | collective-permute-start | bytes 1572872 | tf_op jit(solution)/shard_map/ppermute | solution.py:33
  111.7 15.2 %copy-start.15 = (s32[8]{0:T(128)S(1)}, s32[8]{0:T(128)}, u32[]{:S(2)}) copy-start(s32[8]{0:T(128)} %param.20) | copy-start | bytes 100
  111.7 15.3 %copy-start.2 = (s32[8]{0:T(128)S(1)}, s32[8]{0:T(128)}, u32[]{:S(2)}) copy-start(s32[8]{0:T(128)} %param.19) | copy-start | bytes 100
  111.8 15.9 %copy-start.3 = (s32[8]{0:T(128)S(1)}, s32[8]{0:T(128)}, u32[]{:S(2)}) copy-start(s32[8]{0:T(128)} %param.18) | copy-start | bytes 100
  111.8 16.6 %copy-start.13 = (bf16[2048]{0:T(1024)(128)(2,1)S(1)}, bf16[2048]{0:T(1024)(128)(2,1)}, u32[]{:S(2)}) copy-start(bf16[2048]{0:T(1024)(128)(2,1)} %param.21) | copy-start | bytes 12292
  111.8 62.6 %all-to-all-start.1 = ((bf16[2,8,256,4,128]{4,2,3,0,1:T(8,128)(2,1)}), bf16[2,8,256,4,128]{4,2,3,0,1:T(8,128)(2,1)}, u32[]{:S(2)}, u32[]{:S(2)}) async-start(bf16[2,8,256,4,128]{4,2,3,0,1:T(8,128)(2,1)} %copy.39), calls=%async_computation.1 | async-start | bytes 8388608 | tf_op jit(solution)/shard_map/all_to_all | solution.py:117
  126.9 181.4 %reduce-scatter.7.cloned.1.call-start = ((), (), s32[]{:S(2)}) async-start(), calls=%async_computation.7 | async-start | bytes 2359296
  183.4 2.2 copy-start.4
  187.2 2.8 copy-start.16
  189.0 0.9 copy-start.11
  189.9 2.3 copy-start.12
  192.3 2.4 copy-start.10
  196.7 2.4 copy-start.9
  207.2 0.7 copy-start.14
  207.2 102.2 %copy-start.7 = (bf16[8,8,2048]{2,1,0:T(8,128)(2,1)S(1)}, bf16[8,8,2048]{2,1,0:T(8,128)(2,1)}, u32[]{:S(2)}) copy-start(bf16[8,8,2048]{2,1,0:T(8,128)(2,1)} %copy-done.6) | copy-start | bytes 786436
  207.2 152.9 %all-gather.5.cloned.1.call-start = ((), (), s32[]{:S(2)}) async-start(), calls=%async_computation.6 | async-start | bytes 2359296 | tf_op jit(solution)/shard_map/all_gather | solution.py:155
  311.0 136.3 %reduce-scatter.9.cloned.1.call-start = ((), (), s32[]{:S(2)}) async-start(), calls=%async_computation.8 | async-start | bytes 2359296
  449.4 13.4 %all-to-all-start.2 = ((bf16[2,4,8,2048]{3,2,0,1:T(8,128)(2,1)}), bf16[2,4,8,2048]{3,2,0,1:T(8,128)(2,1)S(1)}, u32[]{:S(2)}, u32[]{:S(2)}) async-start(bf16[2,4,8,2048]{3,2,0,1:T(8,128)(2,1)} %select_convert_fusion), calls=%async_computation.2 | async-start | bytes 524288 | tf_op jit(solution)/shard_map/all_to_all | solution.py:177
  455.2 10.6 %copy-start.1 = (bf16[2048,4,192]{0,2,1:T(8,128)(2,1)S(1)}, bf16[2048,4,192]{0,2,1:T(8,128)(2,1)}, u32[]{:S(2)}) copy-start(bf16[2048,4,192]{0,2,1:T(8,128)(2,1)} %param.22) | copy-start | bytes 9437188
  462.8 0.7 copy-start.8
Sparse Core Ops, SparseCore 0:
  43.1 99.5 all-gather.2
  207.4 100.8 reduce-scatter.6
  311.1 48.9 all-gather.4
  381.8 65.4 reduce-scatter.8
